TPU v7x, 128 devices: a whole 4x4x4 slice. The times are simulated.
128 devices in a mesh: gx: 8 (over z, core), gy: 4 (over x), gz: 4 (over y).
Axes of the slice: x: 4, y: 4, z: 4, core: 2. Of those that a mesh axis runs over, the one named last changes fastest.
Arguments:
- residual_eq: float32 [3, 128, 128, 512], P(None, 'gx', 'gy', 'gz'), may hold values from -6 to 6
- diag_block: float32 [3, 3, 128, 128, 512], P(None, None, 'gx', 'gy', 'gz'), may hold values from -0.6 to 8, as said below
- mobility: float32 [3, 128, 128, 512], P(None, 'gx', 'gy', 'gz'), may hold values from 0.1 to 1
- trans: float32 [3, 128, 128, 512], P(None, 'gx', 'gy', 'gz'), may hold values from 3 to 3000
- perf_cell: int32 [65536], P(('gx', 'gy', 'gz')), may hold values from 0 to 65535
- perf_well: int32 [65536, 1], P(('gx', 'gy', 'gz')), may hold values from 0 to 2559, as said below
- perf_index: float32 [65536], P(('gx', 'gy', 'gz')), may hold values from 10 to 1000
Outputs:
- newton_update: float32 [3, 128, 128, 512], P(None, 'gx', 'gy', 'gz')
Inputs may be any that keep to these rules, and one draw needn't show every extreme that they name: `diag_block`: in every 3 x 3 block the off-diagonal entries lie within -0.6 to 0.6 and the diagonal ones within 2 to 8. `perf_well`: every well has at least one perforation slot; all slots of well w lie on device number w // 20 or on the device after it along gz (number w // 20 + 1, same gx and gy).
All inputs are finite; a program needn't handle non-finite values.
Results may differ from a plain program's by a relative error of at most 0.0003.
Values sent between devices are 32-bit elements; how exact they have to be, the bound alone decides.
No kernel may reach another device: no remote copies, remote signals or barrier semaphores. Data moves between devices by JAX's collectives and lax.ppermute only.
A program may use at most 64 MiB of HBM per device.

v0:
```python
import jax
import jax.numpy as jnp
from jax import lax
from jax.sharding import PartitionSpec as P

WELL_DEV = 20
CSWEEPS = 4
FSWEEPS = 6


omega_fine = 0.7
omega_coarse = 0.7


def from_behind(block, axis, distance):
    devices = range(lax.axis_size(axis))
    route = [(i - distance, i) for i in devices if i - distance in devices]
    return lax.ppermute(block, axis, route)


def padded_2(array, sides, width):
    for axis, dim in sides:
        size, length = (lax.axis_size(axis), array.shape[dim])
        up = [(i, (i + 1) % size) for i in range(size - 1)]
        down = [(j, i) for i, j in up]
        last = lax.slice_in_dim(array, length - width, length, axis=dim)
        leading = lax.slice_in_dim(array, 0, width, axis=dim)
        before = lax.ppermute(last, axis, up)
        after = lax.ppermute(leading, axis, down)
        array = jnp.concatenate([before, array, after], axis=dim)
    return array


def block_solve(blocks, rhs):
    matrix = [[blocks[i, j] for j in range(3)] for i in range(3)]

    def cofactor(i, j):
        return (
            matrix[(i + 1) % 3][(j + 1) % 3] * matrix[(i + 2) % 3][(j + 2) % 3]
            - matrix[(i + 1) % 3][(j + 2) % 3] * matrix[(i + 2) % 3][(j + 1) % 3]
        )

    cofs = [[cofactor(i, j) for j in range(3)] for i in range(3)]
    determinant = matrix[0][0] * cofs[0][0] + matrix[0][1] * cofs[0][1] + matrix[0][2] * cofs[0][2]
    return jnp.stack(
        [
            (cofs[0][j] * rhs[0] + cofs[1][j] * rhs[1] + cofs[2][j] * rhs[2]) / determinant
            for j in range(3)
        ]
    )


def face_flux(field, padded, trans, back):
    total = trans[0] * (field - padded[2:, 1:-1, 1:-1]) + back[0] * (
        field - padded[:-2, 1:-1, 1:-1]
    )
    total = (
        total
        + trans[1] * (field - padded[1:-1, 2:, 1:-1])
        + back[1] * (field - padded[1:-1, :-2, 1:-1])
    )
    total = (
        total
        + trans[2] * (field - padded[1:-1, 1:-1, 2:])
        + back[2] * (field - padded[1:-1, 1:-1, :-2])
    )
    return total


def coarse_step(coarse, rhs_total, coefs, padded):
    dsum, plus_x, minus_x, plus_y, minus_y, plus_z, minus_z, cdiag = coefs
    applied = (
        dsum * coarse
        + plus_x * (coarse - padded[2:, 1:-1, 1:-1])
        + minus_x * (coarse - padded[:-2, 1:-1, 1:-1])
    )
    applied = (
        applied
        + plus_y * (coarse - padded[1:-1, 2:, 1:-1])
        + minus_y * (coarse - padded[1:-1, :-2, 1:-1])
    )
    applied = (
        applied
        + plus_z * (coarse - padded[1:-1, 1:-1, 2:])
        + minus_z * (coarse - padded[1:-1, 1:-1, :-2])
    )
    return coarse + omega_coarse * (rhs_total - applied) / cdiag


def least_squares(beta, h11, h21, h12, h22, h32):
    r11 = jnp.sqrt(h11 * h11 + h21 * h21)
    cos_one = h11 / r11
    sin_one = h21 / r11
    g_first = cos_one * beta
    g_second = -sin_one * beta
    upper = cos_one * h12 + sin_one * h22
    lower = cos_one * h22 - sin_one * h12
    r22 = jnp.sqrt(lower * lower + h32 * h32)
    second = lower * g_second / (r22 * r22)
    first = (g_first - upper * second) / r11
    return (first, second)


def shards(residual_eq, diag_block, mobility, trans, perf_cell, perf_well, perf_index):
    size_x = lax.axis_size("gx")
    size_y = lax.axis_size("gy")
    size_z = lax.axis_size("gz")
    nwells = WELL_DEV * size_x * size_y * size_z
    layer_x = from_behind(trans[0, -1:], "gx", 1)
    layer_y = from_behind(trans[1][:, -1:], "gy", 1)
    layer_z = from_behind(trans[2][:, :, -1:], "gz", 1)
    back = jnp.stack(
        [
            jnp.concatenate([layer_x, trans[0, :-1]], 0),
            jnp.concatenate([layer_y, trans[1][:, :-1]], 1),
            jnp.concatenate([layer_z, trans[2][:, :, :-1]], 2),
        ]
    )
    well_ids = perf_well[:, 0]
    rhs = -residual_eq
    local_square = jnp.sum(rhs * rhs)
    weights, beta_square = lax.psum(
        (jax.ops.segment_sum(perf_index, well_ids, num_segments=nwells), local_square),
        ("gx", "gy", "gz"),
    )
    beta = jnp.sqrt(beta_square)

    def wells(field):
        flat = field.reshape(-1)
        values = flat[perf_cell]
        partial_value = jax.ops.segment_sum(perf_index * values, well_ids, num_segments=nwells)
        bottom = (lax.psum(partial_value, ("gx", "gy", "gz")) / weights)[well_ids]
        terms = perf_index * (values - bottom)
        return jnp.zeros_like(flat).at[perf_cell].add(terms).reshape(field.shape)

    def flux(field):
        padded = padded_2(field, (("gx", 0), ("gy", 1), ("gz", 2)), 1)
        return face_flux(field, padded, trans, back)

    def jacobian(vector):
        coupling = flux(vector[0]) + wells(vector[0])
        return (
            diag_block[:, 0] * vector[0]
            + diag_block[:, 1] * vector[1]
            + diag_block[:, 2] * vector[2]
            + mobility * coupling[None]
        )

    dpress = diag_block[0, 0] + diag_block[1, 0] + diag_block[2, 0]
    lam = mobility[0] + mobility[1] + mobility[2]
    pdiag = dpress + lam * (trans[0] + back[0] + trans[1] + back[1] + trans[2] + back[2])
    dsum = jnp.sum(dpress)
    plus_x = jnp.sum(lam[-1] * trans[0, -1])
    minus_x = jnp.sum(lam[0] * back[0, 0])
    plus_y = jnp.sum(lam[:, -1] * trans[1][:, -1])
    minus_y = jnp.sum(lam[:, 0] * back[1][:, 0])
    plus_z = jnp.sum(lam[:, :, -1] * trans[2][:, :, -1])
    minus_z = jnp.sum(lam[:, :, 0] * back[2][:, :, 0])
    cdiag = dsum + plus_x + minus_x + plus_y + minus_y + plus_z + minus_z
    local_coefs = (dsum, plus_x, minus_x, plus_y, minus_y, plus_z, minus_z, cdiag)
    cell_coefs = tuple((value.reshape(1, 1, 1) for value in local_coefs))

    def smooth(press, rpress):
        for sweep in range(FSWEEPS):
            press = press + omega_fine * (rpress - (dpress * press + lam * flux(press))) / pdiag
        return press

    def coarse_solve(rhs_local):
        rhs_cell = rhs_local.reshape(1, 1, 1)
        coarse = jnp.zeros((1, 1, 1), jnp.float32)
        for sweep in range(CSWEEPS):
            padded = padded_2(coarse, (("gx", 0), ("gy", 1), ("gz", 2)), 1)
            coarse = coarse_step(coarse, rhs_cell, cell_coefs, padded)
        return coarse[0, 0, 0]

    def precondition(vector):
        rpress = vector[0] + vector[1] + vector[2]
        coarse = coarse_solve(jnp.sum(rpress))
        press = smooth(jnp.broadcast_to(coarse, rpress.shape), rpress)
        coupling = flux(press) + wells(press)
        applied = diag_block[:, 0] * press + mobility * coupling[None]
        correction = block_solve(diag_block, vector - applied)
        return jnp.concatenate([(correction[0] + press)[None], correction[1:]], 0)

    def orthogonalize(work, basis):
        products = [jnp.sum(vector * work) for vector in basis]
        totals = lax.psum(jnp.stack(products), ("gx", "gy", "gz"))
        factors = [totals[k] for k in range(len(basis))]
        for vector, factor in zip(basis, factors):
            work = work - factor * vector
        length = jnp.sqrt(lax.psum(jnp.sum(work * work), ("gx", "gy", "gz")))
        return (work, factors, length)

    first_basis = rhs / beta
    first_dir = precondition(first_basis)
    work, factors, h21 = orthogonalize(jacobian(first_dir), [first_basis])
    h11 = factors[0]
    second_basis = work / h21
    second_dir = precondition(second_basis)
    work, factors, h32 = orthogonalize(jacobian(second_dir), [first_basis, second_basis])
    first, second = least_squares(beta, h11, h21, factors[0], factors[1], h32)
    return first * first_dir + second * second_dir


def solution(mesh):
    in_specs = (
        P(None, "gx", "gy", "gz"),
        P(None, None, "gx", "gy", "gz"),
        P(None, "gx", "gy", "gz"),
        P(None, "gx", "gy", "gz"),
        P(("gx", "gy", "gz")),
        P(("gx", "gy", "gz"), None),
        P(("gx", "gy", "gz")),
    )
    out_specs = P(None, "gx", "gy", "gz")
    return jax.shard_map(shards, mesh=mesh, in_specs=in_specs, out_specs=out_specs, check_vma=False)
```

profile of v0, /device:TPU:1, one launch (start us, length us, event | category | flops | bytes accessed | tf_op | source)
XLA Modules:
  0.0 1363.9 jit_solution(7028304365198155474)
XLA Ops:
  4.4 4.6 collective-permute-start.2
  22.9 64.1 %psum.70 = f32[]{:T(128)} all-reduce(f32[]{:T(128)} %multiply_reduce_fusion.5), channel_id=1, replica_groups=mesh['gx'=8,'gy'=4,'gz'=4] {'gx','gy','gz'}, use_global_device_ids=true, to_apply=%region_1.0 | all-reduce | flops 1 | bytes 8 | tf_op jit(solution)/shard_map/psum | solution.py:122
  161.1 6.2 collective-permute-start.16
  195.5 6.3 collective-permute-start.22
  228.5 5.1 collective-permute-start.28
  244.2 5.8 collective-permute-done.32
  273.3 6.6 collective-permute-done.38
  301.1 6.7 collective-permute-done.44
  328.5 6.0 collective-permute-done.50
  355.9 5.6 collective-permute-done.56
  383.5 5.6 collective-permute-done.62
  417.5 63.9 %all-reduce.4 = (f32[2560]{0:T(1024)S(1)}, f32[2560]{0:T(1024)S(1)}) all-reduce(f32[2560]{0:T(1024)S(1)} %scatter_custom_fusion, f32[2560]{0:T(1024)S(1)} %scatter_custom_fusion.1), channel_id=1, replica_groups=mesh['gx'=8,'gy'=4,'gz'=4] {'gx','gy','gz'}, use_global_device_ids=true, to_apply=%region_11.0 | all-reduce | flops 5120 | bytes 40960 | tf_op jit(solution)/shard_map/psum | solution.py:132
  495.5 4.6 collective-permute-done.67
  525.0 63.4 %psum.73 = f32[2560]{0:T(1024)S(1)} all-reduce(f32[2560]{0:T(1024)S(1)} %scatter_custom_fusion.3), channel_id=1, replica_groups=mesh['gx'=8,'gy'=4,'gz'=4] {'gx','gy','gz'}, use_global_device_ids=true, to_apply=%region_16.0 | all-reduce | flops 2560 | bytes 20480 | tf_op jit(solution)/shard_map/psum | solution.py:132
  601.9 4.6 collective-permute-done.73
  611.1 63.6 %psum.74 = f32[]{:T(128)} all-reduce(f32[]{:T(128)} %get-tuple-element.18), channel_id=1, replica_groups=mesh['gx'=8,'gy'=4,'gz'=4] {'gx','gy','gz'}, use_global_device_ids=true, to_apply=%region_19.0 | all-reduce | flops 1 | bytes 8 | tf_op jit(solution)/shard_map/psum | solution.py:187
  677.3 63.0 %psum.75 = f32[]{:T(128)} all-reduce(f32[]{:T(128)} %multiply_reduce_fusion.3), channel_id=1, replica_groups=mesh['gx'=8,'gy'=4,'gz'=4] {'gx','gy','gz'}, use_global_device_ids=true, to_apply=%region_21.0 | all-reduce | flops 1 | bytes 8 | tf_op jit(solution)/shard_map/psum | solution.py:191
  781.7 6.3 collective-permute-start.82
  816.0 6.4 collective-permute-start.88
  849.1 5.2 collective-permute-start.94
  864.9 5.8 collective-permute-done.98
  892.9 7.1 collective-permute-done.104
  921.1 6.0 collective-permute-done.110
  947.8 5.7 collective-permute-done.116
  974.8 5.6 collective-permute-done.122
  1001.8 5.6 collective-permute-done.128
  1031.7 63.7 %psum.76 = f32[2560]{0:T(1024)S(1)} all-reduce(f32[2560]{0:T(1024)S(1)} %scatter_custom_fusion.5), channel_id=1, replica_groups=mesh['gx'=8,'gy'=4,'gz'=4] {'gx','gy','gz'}, use_global_device_ids=true, to_apply=%region_24.0 | all-reduce | flops 2560 | bytes 20480 | tf_op jit(solution)/shard_map/psum | solution.py:132
  1109.5 4.6 collective-permute-done.133
  1141.8 62.8 %psum.77 = f32[2560]{0:T(1024)S(1)} all-reduce(f32[2560]{0:T(1024)S(1)} %scatter_custom_fusion.7), channel_id=1, replica_groups=mesh['gx'=8,'gy'=4,'gz'=4] {'gx','gy','gz'}, use_global_device_ids=true, to_apply=%region_27.0 | all-reduce | flops 2560 | bytes 20480 | tf_op jit(solution)/shard_map/psum | solution.py:132
  1218.8 4.6 collective-permute-done.139
  1229.6 63.6 %psum.78 = f32[2]{0:T(128)S(1)} all-reduce(f32[2]{0:T(128)S(1)} %pad_maximum_fusion.365), channel_id=1, replica_groups=mesh['gx'=8,'gy'=4,'gz'=4] {'gx','gy','gz'}, use_global_device_ids=true, to_apply=%region_31.0 | all-reduce | flops 2 | bytes 16 | tf_op jit(solution)/shard_map/psum | solution.py:187
  1299.3 62.5 %psum.79 = f32[]{:T(128)} all-reduce(f32[]{:T(128)} %multiply_reduce_fusion), channel_id=1, replica_groups=mesh['gx'=8,'gy'=4,'gz'=4] {'gx','gy','gz'}, use_global_device_ids=true, to_apply=%region_33.0 | all-reduce | flops 1 | bytes 8 | tf_op jit(solution)/shard_map/psum | solution.py:191
  (509 shorter events, 583.9 us)
Async XLA Ops:
  0.0 91.9 %collective-permute-start = (f32[1,1,1]{0,2,1:T(1,128)}, f32[1,1,1]{0,2,1:T(1,128)}, u32[]{:S(2)}, u32[]{:S(2)}) collective-permute-start(f32[1,1,1]{0,2,1:T(1,128)} %constant.8.clone.1), channel_id=1, source_target_pairs={{16,0},{32,16},{48,32},{64,48},{80,64},{96,80},{112,96},{17,1},{33... | collective-permute-start | bytes 20 | tf_op jit(solution)/shard_map/ppermute | solution.py:29
  4.4 87.6 %collective-permute-start.2 = (f32[1,1,1]{0,2,1:T(1,128)}, f32[1,1,1]{0,2,1:T(1,128)}, u32[]{:S(2)}, u32[]{:S(2)}) collective-permute-start(f32[1,1,1]{0,2,1:T(1,128)} %constant.8.clone.1), channel_id=1, source_target_pairs={{0,16},{16,32},{32,48},{48,64},{64,80},{80,96},{96,112},{1,17},{17... | collective-permute-start | bytes 20 | tf_op jit(solution)/shard_map/ppermute | solution.py:28
  9.7 106.4 %collective-permute-start.1 = (f32[1,32,128]{2,1,0:T(8,128)S(1)}, f32[1,32,128]{2,1,0:T(8,128)S(1)}, u32[]{:S(2)}, u32[]{:S(2)}) collective-permute-start(f32[1,32,128]{2,1,0:T(8,128)S(1)} %slice_bitcast_fusion.3), channel_id=1, source_target_pairs={{0,16},{16,32},{32,48},{48,64},{64,80},{80,96},{96,112},{1,17},{17... | collective-permute-start | bytes 49160 | tf_op jit(solution)/shard_map/ppermute | solution.py:18
  12.9 101.2 %collective-permute-start.4 = (f32[16,1,128]{2,1,0:T(1,128)S(1)}, f32[16,1,128]{2,1,0:T(1,128)S(1)}, u32[]{:S(2)}, u32[]{:S(2)}) collective-permute-start(f32[16,1,128]{2,1,0:T(1,128)S(1)} %slice.1265), channel_id=1, source_target_pairs={{0,4},{4,8},{8,12},{1,5},{5,9},{9,13},{2,6},{6,10},{10,14},{3,7},{... | collective-permute-start | bytes 24584 | tf_op jit(solution)/shard_map/ppermute | solution.py:18
  17.0 94.0 %collective-permute-start.7 = (f32[16,32,1]{2,1,0:T(8,128)}, f32[16,32,1]{2,1,0:T(8,128)}, u32[]{:S(2)}, u32[]{:S(2)}) collective-permute-start(f32[16,32,1]{2,1,0:T(8,128)} %slice.1268), channel_id=1, source_target_pairs={{0,1},{1,2},{2,3},{4,5},{5,6},{6,7},{8,9},{9,10},{10,11},{12,13},{... | collective-permute-start | bytes 6152 | tf_op jit(solution)/shard_map/ppermute | solution.py:18
  145.0 10.0 collective-permute-start.14
  242.9 11.2 collective-permute-start.31
  269.8 10.1 collective-permute-start.38
  272.0 12.2 collective-permute-start.37
  299.8 11.9 collective-permute-start.43
  327.2 11.2 collective-permute-start.49
  354.6 10.7 collective-permute-start.55
  382.0 10.9 collective-permute-start.61
  400.5 84.1 %collective-permute-start.65 = (f32[18,1,128]{2,1,0:T(1,128)S(1)}, f32[18,1,128]{2,1,0:T(1,128)S(1)}, u32[]{:S(2)}, u32[]{:S(2)}) collective-permute-start(f32[18,1,128]{2,1,0:T(1,128)S(1)} %get-tuple-element.95), channel_id=1, source_target_pairs={{4,0},{8,4},{12,8},{5,1},{9,5},{13,9},{6,2},{10,6},{14,10},{7,3},{... | collective-permute-start | bytes 27656 | tf_op jit(solution)/shard_map/ppermute | solution.py:29
  401.8 82.8 %collective-permute-start.66 = (f32[18,1,128]{2,1,0:T(1,128)S(1)}, f32[18,1,128]{2,1,0:T(1,128)S(1)}, u32[]{:S(2)}, u32[]{:S(2)}) collective-permute-start(f32[18,1,128]{2,1,0:T(1,128)S(1)} %get-tuple-element.94), channel_id=1, source_target_pairs={{0,4},{4,8},{8,12},{1,5},{5,9},{9,13},{2,6},{6,10},{10,14},{3,7},{... | collective-permute-start | bytes 27656 | tf_op jit(solution)/shard_map/ppermute | solution.py:28
  489.1 11.0 collective-permute-start.67
  511.3 80.4 %collective-permute-start.71 = (f32[18,1,128]{2,1,0:T(1,128)S(1)}, f32[18,1,128]{2,1,0:T(1,128)S(1)}, u32[]{:S(2)}, u32[]{:S(2)}) collective-permute-start(f32[18,1,128]{2,1,0:T(1,128)S(1)} %get-tuple-element.93), channel_id=1, source_target_pairs={{4,0},{8,4},{12,8},{5,1},{9,5},{13,9},{6,2},{10,6},{14,10},{7,3},{... | collective-permute-start | bytes 27656 | tf_op jit(solution)/shard_map/ppermute | solution.py:29
  512.6 79.1 %collective-permute-start.72 = (f32[18,1,128]{2,1,0:T(1,128)S(1)}, f32[18,1,128]{2,1,0:T(1,128)S(1)}, u32[]{:S(2)}, u32[]{:S(2)}) collective-permute-start(f32[18,1,128]{2,1,0:T(1,128)S(1)} %get-tuple-element.92), channel_id=1, source_target_pairs={{0,4},{4,8},{8,12},{1,5},{5,9},{9,13},{2,6},{6,10},{10,14},{3,7},{... | collective-permute-start | bytes 27656 | tf_op jit(solution)/shard_map/ppermute | solution.py:28
  595.4 11.0 collective-permute-start.73
  863.6 11.2 collective-permute-start.97
  888.8 11.1 collective-permute-start.104
  891.6 12.3 collective-permute-start.103
  919.4 11.6 collective-permute-start.109
  946.5 10.9 collective-permute-start.115
  973.5 10.8 collective-permute-start.121
  1000.5 10.7 collective-permute-start.127
  1018.9 79.6 %collective-permute-start.131 = (f32[18,1,128]{2,1,0:T(1,128)S(1)}, f32[18,1,128]{2,1,0:T(1,128)S(1)}, u32[]{:S(2)}, u32[]{:S(2)}) collective-permute-start(f32[18,1,128]{2,1,0:T(1,128)S(1)} %get-tuple-element.79), channel_id=1, source_target_pairs={{4,0},{8,4},{12,8},{5,1},{9,5},{13,9},{6,2},{10,6},{14,10},{7,3},{... | collective-permute-start | bytes 27656 | tf_op jit(solution)/shard_map/ppermute | solution.py:29
  1020.2 78.3 %collective-permute-start.132 = (f32[18,1,128]{2,1,0:T(1,128)S(1)}, f32[18,1,128]{2,1,0:T(1,128)S(1)}, u32[]{:S(2)}, u32[]{:S(2)}) collective-permute-start(f32[18,1,128]{2,1,0:T(1,128)S(1)} %get-tuple-element.78), channel_id=1, source_target_pairs={{0,4},{4,8},{8,12},{1,5},{5,9},{9,13},{2,6},{6,10},{10,14},{3,7},{... | collective-permute-start | bytes 27656 | tf_op jit(solution)/shard_map/ppermute | solution.py:28
  1103.1 11.0 collective-permute-start.133
  1126.5 81.3 %collective-permute-start.137 = (f32[18,1,128]{2,1,0:T(1,128)S(1)}, f32[18,1,128]{2,1,0:T(1,128)S(1)}, u32[]{:S(2)}, u32[]{:S(2)}) collective-permute-start(f32[18,1,128]{2,1,0:T(1,128)S(1)} %get-tuple-element.77), channel_id=1, source_target_pairs={{4,0},{8,4},{12,8},{5,1},{9,5},{13,9},{6,2},{10,6},{14,10},{7,3},{... | collective-permute-start | bytes 27656 | tf_op jit(solution)/shard_map/ppermute | solution.py:29
  1127.8 80.0 %collective-permute-start.138 = (f32[18,1,128]{2,1,0:T(1,128)S(1)}, f32[18,1,128]{2,1,0:T(1,128)S(1)}, u32[]{:S(2)}, u32[]{:S(2)}) collective-permute-start(f32[18,1,128]{2,1,0:T(1,128)S(1)} %get-tuple-element.76), channel_id=1, source_target_pairs={{0,4},{4,8},{8,12},{1,5},{5,9},{9,13},{2,6},{6,10},{10,14},{3,7},{... | collective-permute-start | bytes 27656 | tf_op jit(solution)/shard_map/ppermute | solution.py:28
  1212.1 11.2 collective-permute-start.139
  (141 other events, 1801.3 us)
where the time goes:
time: 1380 us; the launch traced here: 1360 us
  blocking collectives  571 us (41%)
  starting transfers between devices  392 us (28%)
  waiting for transfers between devices  164 us (12%)
  other arithmetic  105 us (8%)
  between operations  78.7 us (6%)
  local copies, waits for them, and re-layouts  54 us (4%)
    psum x4, blocking collectives, wells(): bottom = (lax.psum(partial_value, ('gx', 'gy', 'gz')) / weights)[well_ids]  254 us
    ppermute x69, starting transfers between devices, padded_2(): before = lax.ppermute(last, axis, up)  249 us
    ppermute x69, starting transfers between devices, padded_2(): after = lax.ppermute(leading, axis, down)  134 us
    psum x2, blocking collectives, orthogonalize(): totals = lax.psum(jnp.stack(products), ('gx', 'gy', 'gz'))  127 us
    psum x2, blocking collectives, orthogonalize(): length = jnp.sqrt(lax.psum(jnp.sum(work * work), ('gx', 'gy', 'gz')))  126 us
    ppermute x69, waiting for transfers between devices, padded_2(): before = lax.ppermute(last, axis, up)  97.9 us
    ppermute x69, waiting for transfers between devices, padded_2(): after = lax.ppermute(leading, axis, down)  65.7 us
    psum x1, blocking collectives, shards(): lax.psum((jax.ops.segment_sum(perf_index, well_ids, num_segments=nwells),...  64.1 us
  transfers between devices with their start and end apart: 141, of which 58 were waited for; matrix products, arithmetic and copies ran while one was open for 7% of the time, Pallas kernels for 0%

commit v1 on v0

v1 whole, which is shorter than its diff:
```python
import jax
import jax.numpy as jnp
from jax import lax
from jax.sharding import PartitionSpec as P

WELL_DEV = 20
CSWEEPS = 4
FSWEEPS = 6


omega_fine = 0.7
omega_coarse = 0.7

AXES = ("gx", "gy", "gz")


def send_up(block, axis):
    size = lax.axis_size(axis)
    return lax.ppermute(block, axis, [(i, i + 1) for i in range(size - 1)])


def send_down(block, axis):
    size = lax.axis_size(axis)
    return lax.ppermute(block, axis, [(i + 1, i) for i in range(size - 1)])


def allsum(value):
    for axis in reversed(AXES):
        size = lax.axis_size(axis)
        if size & (size - 1):
            value = lax.psum(value, axis)
            continue
        step = 1
        while step < size:
            value = value + lax.ppermute(value, axis, [(i, i ^ step) for i in range(size)])
            step *= 2
    return value


def device_number():
    return (lax.axis_index("gx") * lax.axis_size("gy") + lax.axis_index("gy")) * lax.axis_size(
        "gz"
    ) + lax.axis_index("gz")


def gather_all(local):
    count = lax.axis_size("gx") * lax.axis_size("gy") * lax.axis_size("gz")
    slots = jnp.zeros((count, local.shape[0]), local.dtype).at[device_number()].set(local)
    return allsum(slots)


def block_solve(blocks, rhs):
    matrix = [[blocks[i, j] for j in range(3)] for i in range(3)]

    def cofactor(i, j):
        return (
            matrix[(i + 1) % 3][(j + 1) % 3] * matrix[(i + 2) % 3][(j + 2) % 3]
            - matrix[(i + 1) % 3][(j + 2) % 3] * matrix[(i + 2) % 3][(j + 1) % 3]
        )

    cofs = [[cofactor(i, j) for j in range(3)] for i in range(3)]
    determinant = matrix[0][0] * cofs[0][0] + matrix[0][1] * cofs[0][1] + matrix[0][2] * cofs[0][2]
    return jnp.stack(
        [
            (cofs[0][j] * rhs[0] + cofs[1][j] * rhs[1] + cofs[2][j] * rhs[2]) / determinant
            for j in range(3)
        ]
    )


def face_flux(field, faces, trans, back):
    x_next, x_prev, y_next, y_prev, z_next, z_prev = faces
    padded = jnp.pad(field, 1)
    padded = padded.at[-1:, 1:-1, 1:-1].set(x_next)
    padded = padded.at[:1, 1:-1, 1:-1].set(x_prev)
    padded = padded.at[1:-1, -1:, 1:-1].set(y_next)
    padded = padded.at[1:-1, :1, 1:-1].set(y_prev)
    padded = padded.at[1:-1, 1:-1, -1:].set(z_next)
    padded = padded.at[1:-1, 1:-1, :1].set(z_prev)
    total = trans[0] * (field - padded[2:, 1:-1, 1:-1]) + back[0] * (
        field - padded[:-2, 1:-1, 1:-1]
    )
    total = (
        total
        + trans[1] * (field - padded[1:-1, 2:, 1:-1])
        + back[1] * (field - padded[1:-1, :-2, 1:-1])
    )
    total = (
        total
        + trans[2] * (field - padded[1:-1, 1:-1, 2:])
        + back[2] * (field - padded[1:-1, 1:-1, :-2])
    )
    return total


def coarse_step(coarse, rhs_total, coefs, padded):
    dsum, plus_x, minus_x, plus_y, minus_y, plus_z, minus_z, cdiag = coefs
    applied = (
        dsum * coarse
        + plus_x * (coarse - padded[2:, 1:-1, 1:-1])
        + minus_x * (coarse - padded[:-2, 1:-1, 1:-1])
    )
    applied = (
        applied
        + plus_y * (coarse - padded[1:-1, 2:, 1:-1])
        + minus_y * (coarse - padded[1:-1, :-2, 1:-1])
    )
    applied = (
        applied
        + plus_z * (coarse - padded[1:-1, 1:-1, 2:])
        + minus_z * (coarse - padded[1:-1, 1:-1, :-2])
    )
    return coarse + omega_coarse * (rhs_total - applied) / cdiag


def least_squares(beta, h11, h21, h12, h22, h32):
    r11 = jnp.sqrt(h11 * h11 + h21 * h21)
    cos_one = h11 / r11
    sin_one = h21 / r11
    g_first = cos_one * beta
    g_second = -sin_one * beta
    upper = cos_one * h12 + sin_one * h22
    lower = cos_one * h22 - sin_one * h12
    r22 = jnp.sqrt(lower * lower + h32 * h32)
    second = lower * g_second / (r22 * r22)
    first = (g_first - upper * second) / r11
    return (first, second)


def shards(residual_eq, diag_block, mobility, trans, perf_cell, perf_well, perf_index):
    size_x = lax.axis_size("gx")
    size_y = lax.axis_size("gy")
    size_z = lax.axis_size("gz")
    cx, cy, cz = trans.shape[1:]
    ix = lax.axis_index("gx")
    iy = lax.axis_index("gy")
    iz = lax.axis_index("gz")

    local_well = perf_well[:, 0] - (device_number() - 1) * WELL_DEV

    def well_partials(values):
        return jax.ops.segment_sum(values, local_well, num_segments=2 * WELL_DEV)

    def exchange(field, partial):
        x_next = send_down(field[:1], "gx")
        x_prev = send_up(field[-1:], "gx")
        y_next = send_down(field[:, :1], "gy")
        y_prev = send_up(field[:, -1:], "gy")
        down = jnp.concatenate([field[:, :, 0].reshape(-1), partial[:WELL_DEV]])
        up = jnp.concatenate([field[:, :, -1].reshape(-1), partial[WELL_DEV:]])
        from_next = send_down(down, "gz")
        from_prev = send_up(up, "gz")
        z_next = from_next[: cx * cy].reshape(cx, cy, 1)
        z_prev = from_prev[: cx * cy].reshape(cx, cy, 1)
        totals = partial + jnp.concatenate([from_prev[cx * cy :], from_next[cx * cy :]])
        return (x_next, x_prev, y_next, y_prev, z_next, z_prev), totals

    weight_part = well_partials(perf_index)
    faces_t, weights = exchange(trans[2], weight_part)
    layer_x = send_up(trans[0, -1:], "gx")
    layer_y = send_up(trans[1][:, -1:], "gy")
    layer_z = faces_t[5]
    back = jnp.stack(
        [
            jnp.concatenate([layer_x, trans[0, :-1]], 0),
            jnp.concatenate([layer_y, trans[1][:, :-1]], 1),
            jnp.concatenate([layer_z, trans[2][:, :, :-1]], 2),
        ]
    )

    def flux(field, faces):
        return face_flux(field, faces, trans, back)

    def flux_wells(field):
        flat = field.reshape(-1)
        values = flat[perf_cell]
        faces, totals = exchange(field, well_partials(perf_index * values))
        bottom = (totals / weights)[local_well]
        terms = perf_index * (values - bottom)
        wells = jnp.zeros_like(flat).at[perf_cell].add(terms).reshape(field.shape)
        return flux(field, faces) + wells

    def jacobian(vector):
        coupling = flux_wells(vector[0])
        return (
            diag_block[:, 0] * vector[0]
            + diag_block[:, 1] * vector[1]
            + diag_block[:, 2] * vector[2]
            + mobility * coupling[None]
        )

    dpress = diag_block[0, 0] + diag_block[1, 0] + diag_block[2, 0]
    lam = mobility[0] + mobility[1] + mobility[2]
    pdiag = dpress + lam * (trans[0] + back[0] + trans[1] + back[1] + trans[2] + back[2])
    dsum = jnp.sum(dpress)
    plus_x = jnp.sum(lam[-1] * trans[0, -1])
    minus_x = jnp.sum(lam[0] * back[0, 0])
    plus_y = jnp.sum(lam[:, -1] * trans[1][:, -1])
    minus_y = jnp.sum(lam[:, 0] * back[1][:, 0])
    plus_z = jnp.sum(lam[:, :, -1] * trans[2][:, :, -1])
    minus_z = jnp.sum(lam[:, :, 0] * back[2][:, :, 0])

    rhs = -residual_eq
    start = gather_all(
        jnp.stack(
            [
                jnp.sum(rhs * rhs),
                jnp.sum(rhs[0] + rhs[1] + rhs[2]),
                dsum,
                plus_x,
                minus_x,
                plus_y,
                minus_y,
                plus_z,
                minus_z,
            ]
        )
    )
    grid = (size_x, size_y, size_z)
    beta = jnp.sqrt(jnp.sum(start[:, 0]))
    coarse_coefs = [start[:, k].reshape(grid) for k in range(2, 9)]
    cdiag = coarse_coefs[0]
    for value in coarse_coefs[1:]:
        cdiag = cdiag + value
    coarse_coefs = tuple(coarse_coefs) + (cdiag,)

    def coarse_solve(rhs_total):
        coarse = jnp.zeros(grid, jnp.float32)
        for sweep in range(CSWEEPS):
            coarse = coarse_step(coarse, rhs_total, coarse_coefs, jnp.pad(coarse, 1))
        padded = jnp.pad(coarse, 1)

        def at(dx, dy, dz):
            return padded[ix + 1 + dx, iy + 1 + dy, iz + 1 + dz]

        faces = (
            jnp.broadcast_to(at(1, 0, 0), (1, cy, cz)),
            jnp.broadcast_to(at(-1, 0, 0), (1, cy, cz)),
            jnp.broadcast_to(at(0, 1, 0), (cx, 1, cz)),
            jnp.broadcast_to(at(0, -1, 0), (cx, 1, cz)),
            jnp.broadcast_to(at(0, 0, 1), (cx, cy, 1)),
            jnp.broadcast_to(at(0, 0, -1), (cx, cy, 1)),
        )
        return at(0, 0, 0), faces

    def precondition(vector, rhs_total):
        rpress = vector[0] + vector[1] + vector[2]
        own, faces = coarse_solve(rhs_total)
        press = jnp.broadcast_to(own, rpress.shape)
        for sweep in range(FSWEEPS):
            if sweep:
                faces, _ = exchange(press, jnp.zeros((2 * WELL_DEV,), jnp.float32))
            press = press + omega_fine * (rpress - (dpress * press + lam * flux(press, faces))) / pdiag
        coupling = flux_wells(press)
        applied = diag_block[:, 0] * press + mobility * coupling[None]
        correction = block_solve(diag_block, vector - applied)
        return jnp.concatenate([(correction[0] + press)[None], correction[1:]], 0)

    first_basis = rhs / beta
    first_dir = precondition(first_basis, start[:, 1].reshape(grid) / beta)
    work = jacobian(first_dir)
    h11 = allsum(jnp.sum(first_basis * work))
    work = work - h11 * first_basis
    second = gather_all(jnp.stack([jnp.sum(work * work), jnp.sum(work[0] + work[1] + work[2])]))
    h21 = jnp.sqrt(jnp.sum(second[:, 0]))
    second_basis = work / h21
    second_dir = precondition(second_basis, second[:, 1].reshape(grid) / h21)
    work = jacobian(second_dir)
    products = allsum(jnp.stack([jnp.sum(first_basis * work), jnp.sum(second_basis * work)]))
    h12 = products[0]
    h22 = products[1]
    work = work - h12 * first_basis
    work = work - h22 * second_basis
    h32 = jnp.sqrt(allsum(jnp.sum(work * work)))
    first, second = least_squares(beta, h11, h21, h12, h22, h32)
    return first * first_dir + second * second_dir


def solution(mesh):
    in_specs = (
        P(None, "gx", "gy", "gz"),
        P(None, None, "gx", "gy", "gz"),
        P(None, "gx", "gy", "gz"),
        P(None, "gx", "gy", "gz"),
        P(("gx", "gy", "gz")),
        P(("gx", "gy", "gz"), None),
        P(("gx", "gy", "gz")),
    )
    out_specs = P(None, "gx", "gy", "gz")
    return jax.shard_map(shards, mesh=mesh, in_specs=in_specs, out_specs=out_specs, check_vma=False)
```

time: 1380 us -> 1100 us (0.80)
  blocking collectives: 571 us -> 0 us
  local copies, waits for them, and re-layouts: 54 us -> 411 us
  other arithmetic: 105 us -> 246 us
  waiting for transfers between devices: 164 us -> 63.6 us
  between operations: 78.7 us -> 18.6 us
  starting transfers between devices: 392 us -> 342 us
    psum x9 -> x0, blocking collectives: 571 us -> none  [the longest x4 254 us: wells(): bottom = (lax.psum(partial_value, ('gx', 'gy', 'gz')) / weights)[well_ids]]
    scatter x0 -> x98, local copies, waits for them, and re-layouts: none -> 290 us  [the longest x16 65.3 us: face_flux(): padded = padded.at[1:-1, 1:-1, -1:].set(z_next)]
    ppermute x141 -> x123, waiting for transfers between devices: 164 us -> 63.6 us  [the longest x35 42.1 us: allsum(): lax.ppermute(value, axis, [(i, i ^ step) for i in range(size)])]
    mul x8, other arithmetic: 0.04 us -> 82.7 us  [the longest x4 82.6 us: flux_wells(): terms = perf_index * (values - bottom)]
    ppermute x141 -> x123, starting transfers between devices: 392 us -> 342 us  [the longest x45 161 us: send_up(): return lax.ppermute(block, axis, [(i, i + 1) for i in range(size - 1)])]
    add x16 -> x43, other arithmetic: 13.5 us -> 58.2 us  [the longest x12 41.6 us: precondition(): press + omega_fine * (rpress - (dpress * press + lam * flux(press, faces)...]
    another operation x0 -> x80, local copies, waits for them, and re-layouts: none -> 37.2 us
    pad x0 -> x16, local copies, waits for them, and re-layouts: none -> 21.9 us  [face_flux(): padded = jnp.pad(field, 1)]
  transfers between devices with their start and end apart: 141 -> 123, of which waited for: 58 -> 40; matrix products, arithmetic and copies ran while one was open for 7% -> 33% of each run, Pallas kernels for 0% -> 0%
where the time goes in v1:
time: 1100 us; the launch traced here: 1080 us
  local copies, waits for them, and re-layouts  411 us (37%)
  starting transfers between devices  342 us (31%)
  other arithmetic  246 us (22%)
  waiting for transfers between devices  63.6 us (6%)
  between operations  18.6 us (2%)
    ppermute x45, starting transfers between devices, send_up(): return lax.ppermute(block, axis, [(i, i + 1) for i in range(size - 1)])  161 us
    ppermute x35, starting transfers between devices, allsum(): lax.ppermute(value, axis, [(i, i ^ step) for i in range(size)])  94 us
    ppermute x43, starting transfers between devices, send_down(): return lax.ppermute(block, axis, [(i + 1, i) for i in range(size - 1)])  87.5 us
    mul x4, other arithmetic, flux_wells(): terms = perf_index * (values - bottom)  82.6 us
    scatter x16, local copies, waits for them, and re-layouts, face_flux(): padded = padded.at[1:-1, 1:-1, -1:].set(z_next)  65.3 us
    scatter x16, local copies, waits for them, and re-layouts, face_flux(): padded = padded.at[1:-1, :1, 1:-1].set(y_prev)  59.2 us
    scatter x16, local copies, waits for them, and re-layouts, face_flux(): padded = padded.at[1:-1, -1:, 1:-1].set(y_next)  59.2 us
    ppermute x35, waiting for transfers between devices, allsum(): lax.ppermute(value, axis, [(i, i ^ step) for i in range(size)])  42.1 us
  transfers between devices with their start and end apart: 123, of which 40 were waited for; matrix products, arithmetic and copies ran while one was open for 33% of the time, Pallas kernels for 0%

profile of v1, /device:TPU:1, one launch (start us, length us, event | category | flops | bytes accessed | tf_op | source)
XLA Modules:
  0.0 1080.9 jit_solution(18430379531096243747)
XLA Ops:
  0.8 5.0 collective-permute-start
  29.8 5.8 stack.65
  99.8 4.6 collective-permute-start.13
  142.8 4.6 collective-permute-start.19
  193.2 4.6 collective-permute-start.25
  197.9 4.5 collective-permute-start.27
  282.4 4.6 collective-permute-start.37
  287.0 5.6 collective-permute-start.39
  344.1 4.6 collective-permute-start.43
  351.3 4.3 select_select_fusion.3
  356.2 20.4 %fusion.445 = f32[512]{0:T(512)S(1)} fusion(f32[512]{0:T(512)S(1)} %copy-done.39, f32[512]{0:T(512)S(1)} %gather_fusion, pred[512]{0:T(512)(128)(4,1)S(1)} %get-tuple-element.1259, pred[512]{0:T(512)(128)(4,1)S(1)} %get-tuple-element.1258, pred[512]{0:T(512)(128)(4,1)S(1)} %get-tuple-element.1256, pred[512]{0:T(512)(128)(4,1)S(1)} %get-tuple-element.1257, ...), kind=kLoop, calls=%fused_computation.798 | loop fusion | flops 17920 | bytes 25220 | tf_op jit(solution)/shard_map/mul | solution.py:179
  376.6 4.7 scatter_custom_fusion.2
  435.8 4.6 collective-permute-start.50
  443.3 4.4 select_select_fusion.2
  448.0 20.6 %fusion.444 = f32[512]{0:T(512)S(1)} fusion(f32[512]{0:T(512)S(1)} %copy-done.39, f32[512]{0:T(512)S(1)} %copy-done.44, pred[512]{0:T(512)(128)(4,1)S(1)} %copy-done.143, pred[512]{0:T(512)(128)(4,1)S(1)} %copy-done.140, pred[512]{0:T(512)(128)(4,1)S(1)} %copy-done.134, pred[512]{0:T(512)(128)(4,1)S(1)} %copy-done.137, pred[512]{0:T(512)(128)(4,1)S(1)} %copy-done.49, ...), kind=kLoop, calls=%fused_computation.796 | loop fusion | flops 17920 | bytes 25220 | tf_op jit(solution)/shard_map/mul | solution.py:179
  468.6 4.6 scatter_custom_fusion.4
  519.1 7.5 collective-permute-start.57
  555.9 7.2 collective-permute-start.64
  600.0 4.5 broadcast_add_fusion
  604.5 4.5 collective-permute-start.67
  692.2 5.4 fusion.93
  785.7 4.6 fusion.59
  850.9 4.4 collective-permute-start.97
  859.1 4.6 collective-permute-start.100
  865.8 4.3 select_select_fusion.1
  870.5 20.5 %fusion.443 = f32[512]{0:T(512)S(1)} fusion(f32[512]{0:T(512)S(1)} %copy-done.39, f32[512]{0:T(512)S(1)} %gather_fusion.2, pred[512]{0:T(512)(128)(4,1)S(1)} %copy-done.144, pred[512]{0:T(512)(128)(4,1)S(1)} %copy-done.141, pred[512]{0:T(512)(128)(4,1)S(1)} %copy-done.135, pred[512]{0:T(512)(128)(4,1)S(1)} %copy-done.138, pred[512]{0:T(512)(128)(4,1)S(1)} %copy-done.50, ...), kind=kLoop, calls=%fused_computation.794 | loop fusion | flops 17920 | bytes 25220 | tf_op jit(solution)/shard_map/mul | solution.py:179
  891.0 4.7 scatter_custom_fusion.6
  953.2 4.3 select_select_fusion
  957.6 21.2 %fusion.442 = f32[512]{0:T(512)S(1)} fusion(f32[512]{0:T(512)S(1)} %copy-done.39, f32[512]{0:T(512)S(1)} %gather_fusion.3, pred[512]{0:T(512)(128)(4,1)} %copy-done.142, pred[512]{0:T(512)(128)(4,1)} %copy-done.139, pred[512]{0:T(512)(128)(4,1)} %copy-done.133, pred[512]{0:T(512)(128)(4,1)} %copy-done.136, pred[512]{0:T(512)(128)(4,1)S(1)} %copy-done.50, ...), kind=kLoop, calls=%fused_computation.792 | loop fusion | flops 17920 | bytes 25220 | tf_op jit(solution)/shard_map/mul | solution.py:179
  978.8 4.6 scatter_custom_fusion.8
  1027.7 5.0 collective-permute-start.113
  1063.4 7.3 collective-permute-start.120
  (995 shorter events, 840.2 us)
Async XLA Ops:
  0.8 27.5 %collective-permute-start = (f32[1,32,128]{2,1,0:T(8,128)S(1)}, f32[1,32,128]{2,1,0:T(8,128)S(1)}, u32[]{:S(2)}, u32[]{:S(2)}) collective-permute-start(f32[1,32,128]{2,1,0:T(8,128)S(1)} %slice_bitcast_fusion.3), channel_id=1, source_target_pairs={{0,16},{16,32},{32,48},{48,64},{64,80},{80,96},{96,112},{1,17},{17... | collective-permute-start | bytes 49160 | tf_op jit(solution)/shard_map/ppermute | solution.py:19
  91.4 26.7 %collective-permute-start.10 = (f32[1,32,128]{2,1,0:T(8,128)}, f32[1,32,128]{2,1,0:T(8,128)S(1)}, u32[]{:S(2)}, u32[]{:S(2)}) collective-permute-start(f32[1,32,128]{2,1,0:T(8,128)} %get-tuple-element.1355), channel_id=1, source_target_pairs={{16,0},{32,16},{48,32},{64,48},{80,64},{96,80},{112,96},{17,1},{33... | collective-permute-start | bytes 49160 | tf_op jit(solution)/shard_map/ppermute | solution.py:24
  99.8 23.5 %collective-permute-start.13 = (f32[16,1,128]{2,0,1:T(8,128)}, f32[16,1,128]{2,0,1:T(8,128)}, u32[]{:S(2)}, u32[]{:S(2)}) collective-permute-start(f32[16,1,128]{2,0,1:T(8,128)} %bitcast.38), channel_id=1, source_target_pairs={{0,4},{4,8},{8,12},{1,5},{5,9},{9,13},{2,6},{6,10},{10,14},{3,7},{... | collective-permute-start | bytes 24584 | tf_op jit(solution)/shard_map/ppermute | solution.py:19
  142.8 25.0 %collective-permute-start.19 = (f32[16,1,128]{2,0,1:T(8,128)}, f32[16,1,128]{2,0,1:T(8,128)}, u32[]{:S(2)}, u32[]{:S(2)}) collective-permute-start(f32[16,1,128]{2,0,1:T(8,128)} %bitcast.42), channel_id=1, source_target_pairs={{0,4},{4,8},{8,12},{1,5},{5,9},{9,13},{2,6},{6,10},{10,14},{3,7},{... | collective-permute-start | bytes 24584 | tf_op jit(solution)/shard_map/ppermute | solution.py:19
  233.1 24.6 %collective-permute-start.31 = (f32[16,1,128]{2,0,1:T(8,128)}, f32[16,1,128]{2,0,1:T(8,128)S(1)}, u32[]{:S(2)}, u32[]{:S(2)}) collective-permute-start(f32[16,1,128]{2,0,1:T(8,128)} %bitcast.810), channel_id=1, source_target_pairs={{0,4},{4,8},{8,12},{1,5},{5,9},{9,13},{2,6},{6,10},{10,14},{3,7},{... | collective-permute-start | bytes 24584 | tf_op jit(solution)/shard_map/ppermute | solution.py:19
  246.1 36.3 %collective-permute-start.46 = (f32[532]{0:T(1024)}, f32[532]{0:T(1024)S(1)}, u32[]{:S(2)}, u32[]{:S(2)}) collective-permute-start(f32[532]{0:T(1024)} %pad_maximum_fusion.6), channel_id=1, source_target_pairs={{1,0},{2,1},{3,2},{5,4},{6,5},{7,6},{9,8},{10,9},{11,10},{13,12},{... | collective-permute-start | bytes 6392 | tf_op jit(solution)/shard_map/ppermute | solution.py:24
  274.9 24.1 %collective-permute-start.34 = (f32[1,32,128]{2,1,0:T(8,128)}, f32[1,32,128]{2,1,0:T(8,128)}, u32[]{:S(2)}, u32[]{:S(2)}) collective-permute-start(f32[1,32,128]{2,1,0:T(8,128)} %get-tuple-element.1339), channel_id=1, source_target_pairs={{16,0},{32,16},{48,32},{64,48},{80,64},{96,80},{112,96},{17,1},{33... | collective-permute-start | bytes 49160 | tf_op jit(solution)/shard_map/ppermute | solution.py:24
  277.1 24.7 %collective-permute-start.35 = (f32[1,32,128]{2,1,0:T(8,128)}, f32[1,32,128]{2,1,0:T(8,128)}, u32[]{:S(2)}, u32[]{:S(2)}) collective-permute-start(f32[1,32,128]{2,1,0:T(8,128)} %get-tuple-element.1338), channel_id=1, source_target_pairs={{0,16},{16,32},{32,48},{48,64},{64,80},{80,96},{96,112},{1,17},{17... | collective-permute-start | bytes 49160 | tf_op jit(solution)/shard_map/ppermute | solution.py:19
  280.4 24.1 %collective-permute-start.36 = (f32[16,1,128]{2,0,1:T(8,128)}, f32[16,1,128]{2,0,1:T(8,128)}, u32[]{:S(2)}, u32[]{:S(2)}) collective-permute-start(f32[16,1,128]{2,0,1:T(8,128)} %bitcast.52), channel_id=1, source_target_pairs={{4,0},{8,4},{12,8},{5,1},{9,5},{13,9},{6,2},{10,6},{14,10},{7,3},{... | collective-permute-start | bytes 24584 | tf_op jit(solution)/shard_map/ppermute | solution.py:24
  282.4 26.0 %collective-permute-start.37 = (f32[16,1,128]{2,0,1:T(8,128)}, f32[16,1,128]{2,0,1:T(8,128)}, u32[]{:S(2)}, u32[]{:S(2)}) collective-permute-start(f32[16,1,128]{2,0,1:T(8,128)} %bitcast.54), channel_id=1, source_target_pairs={{0,4},{4,8},{8,12},{1,5},{5,9},{9,13},{2,6},{6,10},{10,14},{3,7},{... | collective-permute-start | bytes 24584 | tf_op jit(solution)/shard_map/ppermute | solution.py:19
  337.0 46.4 %collective-permute-start.40 = (f32[1,32,128]{2,1,0:T(8,128)}, f32[1,32,128]{2,1,0:T(8,128)}, u32[]{:S(2)}, u32[]{:S(2)}) collective-permute-start(f32[1,32,128]{2,1,0:T(8,128)} %get-tuple-element.1335), channel_id=1, source_target_pairs={{16,0},{32,16},{48,32},{64,48},{80,64},{96,80},{112,96},{17,1},{33... | collective-permute-start | bytes 49160 | tf_op jit(solution)/shard_map/ppermute | solution.py:24
  340.2 46.0 %collective-permute-start.41 = (f32[1,32,128]{2,1,0:T(8,128)}, f32[1,32,128]{2,1,0:T(8,128)}, u32[]{:S(2)}, u32[]{:S(2)}) collective-permute-start(f32[1,32,128]{2,1,0:T(8,128)} %get-tuple-element.1334), channel_id=1, source_target_pairs={{0,16},{16,32},{32,48},{48,64},{64,80},{80,96},{96,112},{1,17},{17... | collective-permute-start | bytes 49160 | tf_op jit(solution)/shard_map/ppermute | solution.py:19
  342.8 46.2 %collective-permute-start.42 = (f32[16,1,128]{2,0,1:T(8,128)}, f32[16,1,128]{2,0,1:T(8,128)}, u32[]{:S(2)}, u32[]{:S(2)}) collective-permute-start(f32[16,1,128]{2,0,1:T(8,128)} %bitcast.56), channel_id=1, source_target_pairs={{4,0},{8,4},{12,8},{5,1},{9,5},{13,9},{6,2},{10,6},{14,10},{7,3},{... | collective-permute-start | bytes 24584 | tf_op jit(solution)/shard_map/ppermute | solution.py:24
  344.1 48.8 %collective-permute-start.43 = (f32[16,1,128]{2,0,1:T(8,128)}, f32[16,1,128]{2,0,1:T(8,128)}, u32[]{:S(2)}, u32[]{:S(2)}) collective-permute-start(f32[16,1,128]{2,0,1:T(8,128)} %bitcast.58), channel_id=1, source_target_pairs={{0,4},{4,8},{8,12},{1,5},{5,9},{9,13},{2,6},{6,10},{10,14},{3,7},{... | collective-permute-start | bytes 24584 | tf_op jit(solution)/shard_map/ppermute | solution.py:19
  424.0 54.2 %collective-permute-start.47 = (f32[1,32,128]{2,1,0:T(8,128)}, f32[1,32,128]{2,1,0:T(8,128)}, u32[]{:S(2)}, u32[]{:S(2)}) collective-permute-start(f32[1,32,128]{2,1,0:T(8,128)} %get-tuple-element.1331), channel_id=1, source_target_pairs={{16,0},{32,16},{48,32},{64,48},{80,64},{96,80},{112,96},{17,1},{33... | collective-permute-start | bytes 49160 | tf_op jit(solution)/shard_map/ppermute | solution.py:24
  427.4 53.6 %collective-permute-start.48 = (f32[1,32,128]{2,1,0:T(8,128)}, f32[1,32,128]{2,1,0:T(8,128)}, u32[]{:S(2)}, u32[]{:S(2)}) collective-permute-start(f32[1,32,128]{2,1,0:T(8,128)} %get-tuple-element.1330), channel_id=1, source_target_pairs={{0,16},{16,32},{32,48},{48,64},{64,80},{80,96},{96,112},{1,17},{17... | collective-permute-start | bytes 49160 | tf_op jit(solution)/shard_map/ppermute | solution.py:19
  434.5 49.3 %collective-permute-start.49 = (f32[16,1,128]{2,0,1:T(8,128)}, f32[16,1,128]{2,0,1:T(8,128)}, u32[]{:S(2)}, u32[]{:S(2)}) collective-permute-start(f32[16,1,128]{2,0,1:T(8,128)} %bitcast.121), channel_id=1, source_target_pairs={{4,0},{8,4},{12,8},{5,1},{9,5},{13,9},{6,2},{10,6},{14,10},{7,3},{... | collective-permute-start | bytes 24584 | tf_op jit(solution)/shard_map/ppermute | solution.py:24
  435.8 51.9 %collective-permute-start.50 = (f32[16,1,128]{2,0,1:T(8,128)}, f32[16,1,128]{2,0,1:T(8,128)}, u32[]{:S(2)}, u32[]{:S(2)}) collective-permute-start(f32[16,1,128]{2,0,1:T(8,128)} %bitcast.123), channel_id=1, source_target_pairs={{0,4},{4,8},{8,12},{1,5},{5,9},{9,13},{2,6},{6,10},{10,14},{3,7},{... | collective-permute-start | bytes 24584 | tf_op jit(solution)/shard_map/ppermute | solution.py:19
  612.8 23.5 %collective-permute-start.70 = (f32[16,1,128]{2,0,1:T(8,128)S(1)}, f32[16,1,128]{2,0,1:T(8,128)S(1)}, u32[]{:S(2)}, u32[]{:S(2)}) collective-permute-start(f32[16,1,128]{2,0,1:T(8,128)S(1)} %bitcast.812), channel_id=1, source_target_pairs={{0,4},{4,8},{8,12},{1,5},{5,9},{9,13},{2,6},{6,10},{10,14},{3,7},{... | collective-permute-start | bytes 24584 | tf_op jit(solution)/shard_map/ppermute | solution.py:19
  657.6 24.7 %collective-permute-start.76 = (f32[16,1,128]{2,0,1:T(8,128)S(1)}, f32[16,1,128]{2,0,1:T(8,128)S(1)}, u32[]{:S(2)}, u32[]{:S(2)}) collective-permute-start(f32[16,1,128]{2,0,1:T(8,128)S(1)} %bitcast.813), channel_id=1, source_target_pairs={{0,4},{4,8},{8,12},{1,5},{5,9},{9,13},{2,6},{6,10},{10,14},{3,7},{... | collective-permute-start | bytes 24584 | tf_op jit(solution)/shard_map/ppermute | solution.py:19
  705.4 24.6 %collective-permute-start.82 = (f32[16,1,128]{2,0,1:T(8,128)S(1)}, f32[16,1,128]{2,0,1:T(8,128)S(1)}, u32[]{:S(2)}, u32[]{:S(2)}) collective-permute-start(f32[16,1,128]{2,0,1:T(8,128)S(1)} %bitcast.815), channel_id=1, source_target_pairs={{0,4},{4,8},{8,12},{1,5},{5,9},{9,13},{2,6},{6,10},{10,14},{3,7},{... | collective-permute-start | bytes 24584 | tf_op jit(solution)/shard_map/ppermute | solution.py:19
  742.8 23.5 %collective-permute-start.85 = (f32[1,32,128]{2,1,0:T(8,128)S(1)}, f32[1,32,128]{2,1,0:T(8,128)S(1)}, u32[]{:S(2)}, u32[]{:S(2)}) collective-permute-start(f32[1,32,128]{2,1,0:T(8,128)S(1)} %get-tuple-element.1315), channel_id=1, source_target_pairs={{16,0},{32,16},{48,32},{64,48},{80,64},{96,80},{112,96},{17,1},{33... | collective-permute-start | bytes 49160 | tf_op jit(solution)/shard_map/ppermute | solution.py:24
  750.5 25.2 %collective-permute-start.88 = (f32[16,1,128]{2,0,1:T(8,128)S(1)}, f32[16,1,128]{2,0,1:T(8,128)S(1)}, u32[]{:S(2)}, u32[]{:S(2)}) collective-permute-start(f32[16,1,128]{2,0,1:T(8,128)S(1)} %bitcast.814), channel_id=1, source_target_pairs={{0,4},{4,8},{8,12},{1,5},{5,9},{9,13},{2,6},{6,10},{10,14},{3,7},{... | collective-permute-start | bytes 24584 | tf_op jit(solution)/shard_map/ppermute | solution.py:19
  797.9 24.7 %collective-permute-start.94 = (f32[16,1,128]{2,0,1:T(8,128)S(1)}, f32[16,1,128]{2,0,1:T(8,128)S(1)}, u32[]{:S(2)}, u32[]{:S(2)}) collective-permute-start(f32[16,1,128]{2,0,1:T(8,128)S(1)} %bitcast.809), channel_id=1, source_target_pairs={{0,4},{4,8},{8,12},{1,5},{5,9},{9,13},{2,6},{6,10},{10,14},{3,7},{... | collective-permute-start | bytes 24584 | tf_op jit(solution)/shard_map/ppermute | solution.py:19
  850.9 45.3 %collective-permute-start.97 = (f32[1,32,128]{2,1,0:T(8,128)S(1)}, f32[1,32,128]{2,1,0:T(8,128)S(1)}, u32[]{:S(2)}, u32[]{:S(2)}) collective-permute-start(f32[1,32,128]{2,1,0:T(8,128)S(1)} %get-tuple-element.1307), channel_id=1, source_target_pairs={{16,0},{32,16},{48,32},{64,48},{80,64},{96,80},{112,96},{17,1},{33... | collective-permute-start | bytes 49160 | tf_op jit(solution)/shard_map/ppermute | solution.py:24
  855.3 43.6 %collective-permute-start.98 = (f32[1,32,128]{2,1,0:T(8,128)S(1)}, f32[1,32,128]{2,1,0:T(8,128)S(1)}, u32[]{:S(2)}, u32[]{:S(2)}) collective-permute-start(f32[1,32,128]{2,1,0:T(8,128)S(1)} %get-tuple-element.1306), channel_id=1, source_target_pairs={{0,16},{16,32},{32,48},{48,64},{64,80},{80,96},{96,112},{1,17},{17... | collective-permute-start | bytes 49160 | tf_op jit(solution)/shard_map/ppermute | solution.py:19
  857.8 44.0 %collective-permute-start.99 = (f32[16,1,128]{2,0,1:T(8,128)}, f32[16,1,128]{2,0,1:T(8,128)}, u32[]{:S(2)}, u32[]{:S(2)}) collective-permute-start(f32[16,1,128]{2,0,1:T(8,128)} %bitcast.198), channel_id=1, source_target_pairs={{4,0},{8,4},{12,8},{5,1},{9,5},{13,9},{6,2},{10,6},{14,10},{7,3},{... | collective-permute-start | bytes 24584 | tf_op jit(solution)/shard_map/ppermute | solution.py:24
  859.1 46.5 %collective-permute-start.100 = (f32[16,1,128]{2,0,1:T(8,128)}, f32[16,1,128]{2,0,1:T(8,128)}, u32[]{:S(2)}, u32[]{:S(2)}) collective-permute-start(f32[16,1,128]{2,0,1:T(8,128)} %bitcast.200), channel_id=1, source_target_pairs={{0,4},{4,8},{8,12},{1,5},{5,9},{9,13},{2,6},{6,10},{10,14},{3,7},{... | collective-permute-start | bytes 24584 | tf_op jit(solution)/shard_map/ppermute | solution.py:19
  935.1 50.7 %collective-permute-start.103 = (f32[1,32,128]{2,1,0:T(8,128)S(1)}, f32[1,32,128]{2,1,0:T(8,128)S(1)}, u32[]{:S(2)}, u32[]{:S(2)}) collective-permute-start(f32[1,32,128]{2,1,0:T(8,128)S(1)} %get-tuple-element.1303), channel_id=1, source_target_pairs={{16,0},{32,16},{48,32},{64,48},{80,64},{96,80},{112,96},{17,1},{33... | collective-permute-start | bytes 49160 | tf_op jit(solution)/shard_map/ppermute | solution.py:24
  938.1 50.5 %collective-permute-start.104 = (f32[1,32,128]{2,1,0:T(8,128)S(1)}, f32[1,32,128]{2,1,0:T(8,128)S(1)}, u32[]{:S(2)}, u32[]{:S(2)}) collective-permute-start(f32[1,32,128]{2,1,0:T(8,128)S(1)} %get-tuple-element.1302), channel_id=1, source_target_pairs={{0,16},{16,32},{32,48},{48,64},{64,80},{80,96},{96,112},{1,17},{17... | collective-permute-start | bytes 49160 | tf_op jit(solution)/shard_map/ppermute | solution.py:19
  944.4 46.9 %collective-permute-start.105 = (f32[16,1,128]{2,0,1:T(8,128)S(1)}, f32[16,1,128]{2,0,1:T(8,128)S(1)}, u32[]{:S(2)}, u32[]{:S(2)}) collective-permute-start(f32[16,1,128]{2,0,1:T(8,128)S(1)} %bitcast.808), channel_id=1, source_target_pairs={{4,0},{8,4},{12,8},{5,1},{9,5},{13,9},{6,2},{10,6},{14,10},{7,3},{... | collective-permute-start | bytes 24584 | tf_op jit(solution)/shard_map/ppermute | solution.py:24
  945.7 49.5 %collective-permute-start.106 = (f32[16,1,128]{2,0,1:T(8,128)S(1)}, f32[16,1,128]{2,0,1:T(8,128)S(1)}, u32[]{:S(2)}, u32[]{:S(2)}) collective-permute-start(f32[16,1,128]{2,0,1:T(8,128)S(1)} %bitcast.807), channel_id=1, source_target_pairs={{0,4},{4,8},{8,12},{1,5},{5,9},{9,13},{2,6},{6,10},{10,14},{3,7},{... | collective-permute-start | bytes 24584 | tf_op jit(solution)/shard_map/ppermute | solution.py:19
  (257 other events, 4618.4 us)
